TPU v7x, 256 devices: a whole 4x4x8 slice. The times are simulated.
256 devices in a mesh: island: 4 (over x_lo, core), fsdp: 64 (over x_hi, z, y).
Axes of the slice: x: 4 (x_hi: 2, x_lo: 2; x = x_hi * 2 + x_lo), y: 4, z: 8, core: 2. Of those that a mesh axis runs over, the one named last changes fastest.
Arguments:
- acts: bfloat16 [65536, 8192], P(('island', 'fsdp')), may hold values from -24 to 24
- cotangent: bfloat16 [65536, 512], P(('island', 'fsdp')), may hold values from -6 to 6
- global_params: float32 [8192, 512], P('fsdp'), may hold values from -0.12 to 0.12
- momentum: float32 [8192, 512], P('fsdp'), may hold values from -0.18 to 0.18
- island_drift: float32 [4, 8192, 512], P('island', 'fsdp'), may hold values from -0.12 to 0.12
- moment1: float32 [4, 8192, 512], P('island', 'fsdp'), may hold values from -6 to 6
- moment2: float32 [4, 8192, 512], P('island', 'fsdp'), may hold values from 0.05 to 1
Outputs:
- keys: bfloat16 [65536, 512], P(('island', 'fsdp'))
- new_global: float32 [8192, 512], P('fsdp')
- new_momentum: float32 [8192, 512], P('fsdp')
- moment1_out: float32 [4, 8192, 512], P('island', 'fsdp')
- moment2_out: float32 [4, 8192, 512], P('island', 'fsdp')
All inputs are finite; a program needn't handle non-finite values.
Results may differ from a plain program's by a relative error of at most 0.0049.
Values may be sent and summed in bfloat16 or wider, within the bound.
No kernel may reach another device: no remote copies, remote signals or barrier semaphores. Data moves between devices by JAX's collectives and lax.ppermute only.
A program may use at most 128 MiB of HBM per device.

v0:
```python
import jax
import jax.numpy as jnp
from jax import lax
from jax.sharding import PartitionSpec as P

D = 8192
beta_one = 0.9
beta_two = 0.95
epsilon = 1e-08
inner_rate = 0.05
decay_rate = 0.1
outer_rate = 0.7
nesterov = 0.9


def per_device(acts, cotangent, global_params, momentum, island_drift, moment1, moment2):
    fsdp_count = lax.axis_size("fsdp")
    island_count = lax.axis_size("island")
    scale = (acts.shape[0] * fsdp_count) ** (-0.5)
    grad = lax.psum_scatter(
        lax.dot_general(
            acts, cotangent, (((0,), (0,)), ((), ())), preferred_element_type=jnp.float32
        ),
        "fsdp",
        scatter_dimension=0,
        tiled=True,
    )
    grad = grad * scale
    drift = island_drift[0]
    first = beta_one * moment1[0] + (1.0 - beta_one) * grad
    second = beta_two * moment2[0] + (1.0 - beta_two) * grad * grad
    step = first / (jnp.sqrt(second) + epsilon) + decay_rate * (global_params - drift)
    pseudo = drift + inner_rate * step
    mean = lax.psum(pseudo, "island") / island_count
    new_momentum = nesterov * momentum + mean
    new_global = global_params - outer_rate * (mean + nesterov * new_momentum)
    weights = new_global.astype(jnp.bfloat16)
    keys = jnp.dot(
        acts,
        lax.all_gather(weights, "fsdp", axis=0, tiled=True),
        preferred_element_type=jnp.float32,
    )
    keys = (keys * D ** (-0.5)).astype(jnp.bfloat16)
    return (keys, new_global, new_momentum, first[None], second[None])


def solution(mesh):
    return jax.shard_map(
        per_device,
        mesh=mesh,
        in_specs=(
            P(("island", "fsdp"), None),
            P(("island", "fsdp"), None),
            P("fsdp", None),
            P("fsdp", None),
            P("island", "fsdp", None),
            P("island", "fsdp", None),
            P("island", "fsdp", None),
        ),
        out_specs=(
            P(("island", "fsdp"), None),
            P("fsdp", None),
            P("fsdp", None),
            P("island", "fsdp", None),
            P("island", "fsdp", None),
        ),
        check_vma=False,
    )
```

profile of v0, /device:TPU:8, one launch (start us, length us, event | category | flops | bytes accessed | tf_op | source)
XLA Modules:
  0.0 632.4 jit_solution(935737495468121115)
XLA Ops:
  7.2 0.0 copy-start
  7.2 0.0 reduce-scatter.2.cloned.1.call-start
  7.2 0.9 copy-done
  8.1 10.3 %fusion.8 = f32[8192,512]{1,0:T(8,128)} fusion(bf16[256,8192]{1,0:T(8,128)(2,1)} %param.7, bf16[256,512]{1,0:T(8,128)(2,1)S(1)} %copy-done), kind=kOutput, calls=%fused_computation.15 | convolution fusion | flops 2147483648 | bytes 21233664 | tf_op jit(solution)/shard_map/dot_general | solution.py:21
  18.4 0.0 copy-start.1
  18.4 0.0 copy-start.3
  18.4 0.0 copy-start.4
  18.4 0.0 copy-start.5
  18.4 0.0 copy-start.2
  18.5 0.0 reduce-scatter.2.cloned.1.call-update
  18.5 0.0 all-reduce.2.cloned.1.call-start
  18.5 400.2 %reduce-scatter.2.cloned.1.call-done = f32[128,512]{1,0:T(8,128)} async-done(((f32[8192,512]{1,0:T(8,128)}), f32[128,512]{1,0:T(8,128)}) %reduce-scatter.2.cloned.1.call-update) | async-done | bytes 262160 | tf_op jit(solution)/shard_map/reduce_scatter | solution.py:20
  418.8 0.0 copy-done.1
  418.8 0.0 copy-done.3
  418.8 0.0 copy-done.4
  418.8 0.0 copy-done.5
  418.8 2.0 fusion.6
  420.8 0.0 all-reduce.2.cloned.1.call-update
  420.8 0.0 all-gather.2.cloned.1.call-start
  420.9 42.0 %all-reduce.2.cloned.1.call-done = f32[128,512]{1,0:T(8,128)} async-done(((f32[128,512]{1,0:T(8,128)}), f32[128,512]{1,0:T(8,128)}) %all-reduce.2.cloned.1.call-update) | async-done | bytes 262160 | tf_op jit(solution)/shard_map/psum | solution.py:34
  462.9 0.0 copy-done.2
  462.9 1.9 fusion.7
  464.8 0.0 all-gather.2.cloned.1.call-update
  464.8 153.3 %all-gather.2.cloned.1.call-done = bf16[8192,512]{1,0:T(8,128)(2,1)} async-done(((bf16[128,512]{1,0:T(8,128)(2,1)}), bf16[8192,512]{1,0:T(8,128)(2,1)}) %all-gather.2.cloned.1.call-update) | async-done | bytes 8388624 | tf_op jit(solution)/shard_map/all_gather | solution.py:40
  618.1 6.9 %fusion.1 = bf16[256,512]{0,1:T(8,128)(2,1)S(1)} fusion(bf16[8192,512]{1,0:T(8,128)(2,1)} %all-gather.2.cloned.1.call-done, bf16[256,8192]{1,0:T(8,128)(2,1)} %param.7), kind=kOutput, calls=%fused_computation.2 | convolution fusion | flops 2147745792 | bytes 12845056 | tf_op jit(solution)/shard_map/dot_general | solution.py:38
  625.1 0.8 copy.12
Async XLA Ops:
  7.2 1.0 copy-start
  7.2 411.6 %reduce-scatter.2.cloned.1.call-start = ((), (), s32[]{:S(2)}) async-start(), calls=%async_computation.1 | async-start | bytes 17039360 | tf_op jit(solution)/shard_map/reduce_scatter | solution.py:20
  18.4 400.3 %copy-start.1 = (f32[128,512]{1,0:T(8,128)S(1)}, f32[128,512]{1,0:T(8,128)}, u32[]{:S(2)}) copy-start(f32[128,512]{1,0:T(8,128)} %param.9) | copy-start | bytes 786436
  18.4 400.3 %copy-start.3 = (f32[1,128,512]{2,1,0:T(8,128)S(1)}, f32[1,128,512]{2,1,0:T(8,128)}, u32[]{:S(2)}) copy-start(f32[1,128,512]{2,1,0:T(8,128)} %param.13) | copy-start | bytes 786436
  18.4 400.3 %copy-start.4 = (f32[1,128,512]{2,1,0:T(8,128)S(1)}, f32[1,128,512]{2,1,0:T(8,128)}, u32[]{:S(2)}) copy-start(f32[1,128,512]{2,1,0:T(8,128)} %param.12) | copy-start | bytes 786436
  18.4 400.3 %copy-start.5 = (f32[1,128,512]{2,1,0:T(8,128)S(1)}, f32[1,128,512]{2,1,0:T(8,128)}, u32[]{:S(2)}) copy-start(f32[1,128,512]{2,1,0:T(8,128)} %param.11) | copy-start | bytes 786436
  18.4 444.5 %copy-start.2 = (f32[128,512]{1,0:T(8,128)S(1)}, f32[128,512]{1,0:T(8,128)}, u32[]{:S(2)}) copy-start(f32[128,512]{1,0:T(8,128)} %param.10) | copy-start | bytes 786436
  18.5 444.4 %all-reduce.2.cloned.1.call-start = ((), (), s32[]{:S(2)}) async-start(), calls=%async_computation.2 | async-start | bytes 524288 | tf_op jit(solution)/shard_map/psum | solution.py:34
  420.8 197.3 %all-gather.2.cloned.1.call-start = ((), (), s32[]{:S(2)}) async-start(), calls=%async_computation.3 | async-start | bytes 8519680 | tf_op jit(solution)/shard_map/all_gather | solution.py:40
Sparse Core Ops, SparseCore 0:
  18.6 400.1 reduce-scatter.1
  422.0 40.9 all-reduce.1
  467.1 150.9 all-gather.1
where the time goes:
time: 633 us; the launch traced here: 632 us
  waiting for transfers between devices  596 us (94%)
  matrix products  17.3 us (3%)
  between operations  13.8 us (2%)
    reduce_scatter x1, waiting for transfers between devices, per_device(): lax.psum_scatter(lax.dot_general(acts, cotangent, (((0,), (0,)), ((), ())...  400 us
    all_gather x1, waiting for transfers between devices, per_device(): lax.all_gather(weights, 'fsdp', axis=0, tiled=True)  153 us
    psum x1, waiting for transfers between devices, per_device(): mean = lax.psum(pseudo, 'island') / island_count  42 us
  transfers between devices with their start and end apart: 3, of which 3 were waited for; matrix products, arithmetic and copies ran while one was open for 0% of the time, Pallas kernels for 0%

commit v1 on v0

--- a/solution.py
+++ b/solution.py
@@ -31,7 +31,7 @@
     second = beta_two * moment2[0] + (1.0 - beta_two) * grad * grad
     step = first / (jnp.sqrt(second) + epsilon) + decay_rate * (global_params - drift)
     pseudo = drift + inner_rate * step
-    mean = lax.psum(pseudo, "island") / island_count
+    mean = lax.all_gather(pseudo, axis_name="island").sum(axis=0) / island_count
     new_momentum = nesterov * momentum + mean
     new_global = global_params - outer_rate * (mean + nesterov * new_momentum)
     weights = new_global.astype(jnp.bfloat16)

time: 633 us -> 614 us (0.970)
  waiting for transfers between devices: 596 us -> 576 us
    psum x1 -> x0, waiting for transfers between devices: 42 us -> none  [per_device(): mean = lax.psum(pseudo, 'island') / island_count]
    all_gather x0 -> x1, waiting for transfers between devices: none -> 22.7 us  [per_device(): mean = lax.all_gather(pseudo, axis_name='island').sum(axis=0) / island_count]
where the time goes in v1:
time: 614 us; the launch traced here: 613 us
  waiting for transfers between devices  576 us (94%)
  matrix products  17.3 us (3%)
  between operations  13.8 us (2%)
    reduce_scatter x1, waiting for transfers between devices, per_device(): lax.psum_scatter(lax.dot_general(acts, cotangent, (((0,), (0,)), ((), ())...  400 us
    all_gather x1, waiting for transfers between devices, per_device(): lax.all_gather(weights, 'fsdp', axis=0, tiled=True)  153 us
    all_gather x1, waiting for transfers between devices, per_device(): mean = lax.all_gather(pseudo, axis_name='island').sum(axis=0) / island_count  22.7 us
  transfers between devices with their start and end apart: 3, of which 3 were waited for; matrix products, arithmetic and copies ran while one was open for 0% of the time, Pallas kernels for 0%

profile of v1, /device:TPU:8, one launch (start us, length us, event | category | flops | bytes accessed | tf_op | source)
XLA Modules:
  0.0 613.4 jit_solution(15586686653360926640)
XLA Ops:
  7.2 0.0 copy-start
  7.2 0.0 reduce-scatter.2.cloned.1.call-start
  7.2 0.9 copy-done
  8.1 10.3 %fusion.8 = f32[8192,512]{1,0:T(8,128)} fusion(bf16[256,8192]{1,0:T(8,128)(2,1)} %param.7, bf16[256,512]{1,0:T(8,128)(2,1)S(1)} %copy-done), kind=kOutput, calls=%fused_computation.15 | convolution fusion | flops 2147483648 | bytes 21233664 | tf_op jit(solution)/shard_map/dot_general | solution.py:21
  18.4 0.0 copy-start.1
  18.4 0.0 copy-start.3
  18.4 0.0 copy-start.4
  18.4 0.0 copy-start.5
  18.4 0.0 copy-start.2
  18.5 0.0 reduce-scatter.2.cloned.1.call-update
  18.5 0.0 all-gather.6.cloned.1.call-start
  18.5 400.2 %reduce-scatter.2.cloned.1.call-done = f32[128,512]{1,0:T(8,128)} async-done(((f32[8192,512]{1,0:T(8,128)}), f32[128,512]{1,0:T(8,128)}) %reduce-scatter.2.cloned.1.call-update) | async-done | bytes 262160 | tf_op jit(solution)/shard_map/reduce_scatter | solution.py:20
  418.8 0.0 copy-done.1
  418.8 0.0 copy-done.3
  418.8 0.0 copy-done.4
  418.8 0.0 copy-done.5
  418.8 2.0 fusion.6
  420.8 0.0 all-gather.6.cloned.1.call-update
  420.8 0.0 all-gather.4.cloned.1.call-start
  420.9 22.7 %all-gather.6.cloned.1.call-done = f32[512,512]{1,0:T(8,128)} async-done(((f32[128,512]{1,0:T(8,128)}), f32[512,512]{1,0:T(8,128)}) %all-gather.6.cloned.1.call-update) | async-done | bytes 1048592 | tf_op jit(solution)/shard_map/all_gather | solution.py:34
  443.6 1.3 reduce_sum.9
  444.9 0.0 copy-done.2
  444.9 0.9 fusion.7
  445.8 0.0 all-gather.4.cloned.1.call-update
  445.9 153.2 %all-gather.4.cloned.1.call-done = bf16[8192,512]{1,0:T(8,128)(2,1)} async-done(((bf16[128,512]{1,0:T(8,128)(2,1)}), bf16[8192,512]{1,0:T(8,128)(2,1)}) %all-gather.4.cloned.1.call-update) | async-done | bytes 8388624 | tf_op jit(solution)/shard_map/all_gather | solution.py:40
  599.1 6.9 %fusion.1 = bf16[256,512]{0,1:T(8,128)(2,1)S(1)} fusion(bf16[8192,512]{1,0:T(8,128)(2,1)} %all-gather.4.cloned.1.call-done, bf16[256,8192]{1,0:T(8,128)(2,1)} %param.7), kind=kOutput, calls=%fused_computation.2 | convolution fusion | flops 2147745792 | bytes 12845056 | tf_op jit(solution)/shard_map/dot_general | solution.py:38
  606.0 0.8 copy.12
Async XLA Ops:
  7.2 1.0 copy-start
  7.2 411.6 %reduce-scatter.2.cloned.1.call-start = ((), (), s32[]{:S(2)}) async-start(), calls=%async_computation.1 | async-start | bytes 17039360 | tf_op jit(solution)/shard_map/reduce_scatter | solution.py:20
  18.4 400.3 %copy-start.1 = (f32[128,512]{1,0:T(8,128)S(1)}, f32[128,512]{1,0:T(8,128)}, u32[]{:S(2)}) copy-start(f32[128,512]{1,0:T(8,128)} %param.9) | copy-start | bytes 786436
  18.4 400.3 %copy-start.3 = (f32[1,128,512]{2,1,0:T(8,128)S(1)}, f32[1,128,512]{2,1,0:T(8,128)}, u32[]{:S(2)}) copy-start(f32[1,128,512]{2,1,0:T(8,128)} %param.13) | copy-start | bytes 786436
  18.4 400.3 %copy-start.4 = (f32[1,128,512]{2,1,0:T(8,128)S(1)}, f32[1,128,512]{2,1,0:T(8,128)}, u32[]{:S(2)}) copy-start(f32[1,128,512]{2,1,0:T(8,128)} %param.12) | copy-start | bytes 786436
  18.4 400.3 %copy-start.5 = (f32[1,128,512]{2,1,0:T(8,128)S(1)}, f32[1,128,512]{2,1,0:T(8,128)}, u32[]{:S(2)}) copy-start(f32[1,128,512]{2,1,0:T(8,128)} %param.11) | copy-start | bytes 786436
  18.4 426.5 %copy-start.2 = (f32[128,512]{1,0:T(8,128)S(1)}, f32[128,512]{1,0:T(8,128)}, u32[]{:S(2)}) copy-start(f32[128,512]{1,0:T(8,128)} %param.10) | copy-start | bytes 786436
  18.5 425.1 %all-gather.6.cloned.1.call-start = ((), (), s32[]{:S(2)}) async-start(), calls=%async_computation.3 | async-start | bytes 1310720 | tf_op jit(solution)/shard_map/all_gather | solution.py:34
  420.8 178.2 %all-gather.4.cloned.1.call-start = ((), (), s32[]{:S(2)}) async-start(), calls=%async_computation.2 | async-start | bytes 8519680 | tf_op jit(solution)/shard_map/all_gather | solution.py:40
Sparse Core Ops, SparseCore 0:
  18.6 400.1 reduce-scatter.1
  421.2 22.3 all-gather.5
  447.8 151.2 all-gather.3

commit v2 on v0

--- a/solution.py
+++ b/solution.py
@@ -11,6 +11,15 @@
 decay_rate = 0.1
 outer_rate = 0.7
 nesterov = 0.9
+
+
+def define_the_goods(local_values, where_dim):
+    return jnp.concatenate(
+        lax.all_to_all(
+            jnp.stack([local_values] * lax.axis_size("fsdp")), "fsdp", split_axis=0, concat_axis=0
+        ),
+        axis=where_dim,
+    )
 
 
 def per_device(acts, cotangent, global_params, momentum, island_drift, moment1, moment2):
@@ -35,11 +44,7 @@
     new_momentum = nesterov * momentum + mean
     new_global = global_params - outer_rate * (mean + nesterov * new_momentum)
     weights = new_global.astype(jnp.bfloat16)
-    keys = jnp.dot(
-        acts,
-        lax.all_gather(weights, "fsdp", axis=0, tiled=True),
-        preferred_element_type=jnp.float32,
-    )
+    keys = jnp.dot(acts, define_the_goods(weights, 0), preferred_element_type=jnp.float32)
     keys = (keys * D ** (-0.5)).astype(jnp.bfloat16)
     return (keys, new_global, new_momentum, first[None], second[None])
 

time: 633 us -> 677 us (1.070)
  blocking collectives: 0 us -> 199 us
  waiting for transfers between devices: 596 us -> 442 us
    all_to_all x0 -> x1, blocking collectives: none -> 199 us  [define_the_goods(): lax.all_to_all(jnp.stack([local_values] * lax.axis_size('fsdp')), 'fsdp',...]
    all_gather x1 -> x0, waiting for transfers between devices: 153 us -> none  [per_device(): lax.all_gather(weights, 'fsdp', axis=0, tiled=True)]
  transfers between devices with their start and end apart: 3 -> 2, of which waited for: 3 -> 2; matrix products, arithmetic and copies ran while one was open for 0% -> 0% of each run, Pallas kernels for 0% -> 0%
where the time goes in v2:
time: 677 us; the launch traced here: 675 us
  waiting for transfers between devices  442 us (65%)
  blocking collectives  199 us (29%)
  between operations  14.1 us (2%)
  matrix products  12.7 us (2%)
    reduce_scatter x1, waiting for transfers between devices, per_device(): lax.psum_scatter(lax.dot_general(acts, cotangent, (((0,), (0,)), ((), ())...  400 us
    all_to_all x1, blocking collectives, define_the_goods(): lax.all_to_all(jnp.stack([local_values] * lax.axis_size('fsdp')), 'fsdp',...  199 us
    psum x1, waiting for transfers between devices, per_device(): mean = lax.psum(pseudo, 'island') / island_count  42.1 us
  transfers between devices with their start and end apart: 2, of which 2 were waited for; matrix products, arithmetic and copies ran while one was open for 0% of the time, Pallas kernels for 0%

profile of v2, /device:TPU:8, one launch (start us, length us, event | category | flops | bytes accessed | tf_op | source)
XLA Modules:
  0.0 675.1 jit_solution(361592737976531181)
XLA Ops:
  7.2 0.0 copy-start
  7.2 0.0 reduce-scatter.2.cloned.1.call-start
  7.2 0.9 copy-done
  8.1 10.3 %fusion.8 = f32[8192,512]{1,0:T(8,128)} fusion(bf16[256,8192]{1,0:T(8,128)(2,1)} %param.7, bf16[256,512]{1,0:T(8,128)(2,1)S(1)} %copy-done), kind=kOutput, calls=%fused_computation.15 | convolution fusion | flops 2147483648 | bytes 21233664 | tf_op jit(solution)/shard_map/dot_general | solution.py:30
  18.4 0.0 copy-start.2
  18.4 0.0 copy-start.4
  18.4 0.0 copy-start.5
  18.4 0.0 copy-start.6
  18.4 0.0 copy-start.3
  18.4 0.0 reduce-scatter.2.cloned.1.call-update
  18.5 0.0 all-reduce.2.cloned.1.call-start
  18.5 400.2 %reduce-scatter.2.cloned.1.call-done = f32[128,512]{1,0:T(8,128)} async-done(((f32[8192,512]{1,0:T(8,128)}), f32[128,512]{1,0:T(8,128)}) %reduce-scatter.2.cloned.1.call-update) | async-done | bytes 262160 | tf_op jit(solution)/shard_map/reduce_scatter | solution.py:29
  418.8 0.0 copy-done.2
  418.8 0.0 copy-done.4
  418.8 0.0 copy-done.5
  418.8 0.0 copy-done.6
  418.8 2.0 fusion.6
  420.8 0.0 all-reduce.2.cloned.1.call-update
  420.8 42.1 %all-reduce.2.cloned.1.call-done = f32[128,512]{1,0:T(8,128)} async-done(((f32[128,512]{1,0:T(8,128)}), f32[128,512]{1,0:T(8,128)}) %all-reduce.2.cloned.1.call-update) | async-done | bytes 262160 | tf_op jit(solution)/shard_map/psum | solution.py:43
  462.9 0.0 copy-done.3
  462.9 1.8 fusion.7
  464.7 1.0 stack.2
  465.8 0.0 copy-start.1
  465.8 199.2 %all_to_all.5 = bf16[64,128,512]{2,1,0:T(8,128)(2,1)S(1)} all-to-all(bf16[64,128,512]{2,1,0:T(8,128)(2,1)S(1)} %stack.2), channel_id=1, replica_groups=mesh['island'=4,'fsdp'=64] {'fsdp'}, dimensions={0} | all-to-all | bytes 16777216 | tf_op jit(solution)/shard_map/all_to_all | solution.py:18
  665.0 0.0 copy-done.1
  665.0 2.4 fusion.1
  667.4 0.8 copy.12
Async XLA Ops:
  7.2 1.0 copy-start
  7.2 411.6 %reduce-scatter.2.cloned.1.call-start = ((), (), s32[]{:S(2)}) async-start(), calls=%async_computation.2 | async-start | bytes 17039360 | tf_op jit(solution)/shard_map/reduce_scatter | solution.py:29
  18.4 400.3 %copy-start.2 = (f32[128,512]{1,0:T(8,128)S(1)}, f32[128,512]{1,0:T(8,128)}, u32[]{:S(2)}) copy-start(f32[128,512]{1,0:T(8,128)} %param.9) | copy-start | bytes 786436
  18.4 400.3 %copy-start.4 = (f32[1,128,512]{2,1,0:T(8,128)S(1)}, f32[1,128,512]{2,1,0:T(8,128)}, u32[]{:S(2)}) copy-start(f32[1,128,512]{2,1,0:T(8,128)} %param.13) | copy-start | bytes 786436
  18.4 400.3 %copy-start.5 = (f32[1,128,512]{2,1,0:T(8,128)S(1)}, f32[1,128,512]{2,1,0:T(8,128)}, u32[]{:S(2)}) copy-start(f32[1,128,512]{2,1,0:T(8,128)} %param.12) | copy-start | bytes 786436
  18.4 400.3 %copy-start.6 = (f32[1,128,512]{2,1,0:T(8,128)S(1)}, f32[1,128,512]{2,1,0:T(8,128)}, u32[]{:S(2)}) copy-start(f32[1,128,512]{2,1,0:T(8,128)} %param.11) | copy-start | bytes 786436
  18.4 444.5 %copy-start.3 = (f32[128,512]{1,0:T(8,128)S(1)}, f32[128,512]{1,0:T(8,128)}, u32[]{:S(2)}) copy-start(f32[128,512]{1,0:T(8,128)} %param.10) | copy-start | bytes 786436
  18.5 444.4 %all-reduce.2.cloned.1.call-start = ((), (), s32[]{:S(2)}) async-start(), calls=%async_computation.3 | async-start | bytes 524288 | tf_op jit(solution)/shard_map/psum | solution.py:43
  465.8 199.3 %copy-start.1 = (bf16[256,8192]{1,0:T(8,128)(2,1)S(1)}, bf16[256,8192]{1,0:T(8,128)(2,1)}, u32[]{:S(2)}) copy-start(bf16[256,8192]{1,0:T(8,128)(2,1)} %param.7) | copy-start | bytes 12582916
Sparse Core Ops, SparseCore 0:
  18.6 400.1 reduce-scatter.1
  422.0 40.9 all-reduce.1
